TPU v7x, 256 devices: a whole 4x4x8 slice. The times are simulated.
256 devices in a mesh: embed: 8 (over x, core), hidden: 32 (over y, z).
Axes of the slice: x: 4, y: 4, z: 8, core: 2. Of those that a mesh axis runs over, the one named last changes fastest.
Arguments:
- rows_in: bfloat16 [512, 16384], P('hidden', 'embed'), may hold values from -6 to 6
- gate_weight: bfloat16 [16384, 28672], P('embed', 'hidden'), may hold values from -0.046875 to 0.046875
- up_weight: bfloat16 [16384, 28672], P('embed', 'hidden'), may hold values from -0.046875 to 0.046875
- down_weight: bfloat16 [28672, 16384], P('hidden', 'embed'), may hold values from -0.03125 to 0.03125
Outputs:
- rows_out: bfloat16 [512, 16384], P('hidden', 'embed')
All inputs are finite; a program needn't handle non-finite values.
Results may differ from a plain program's by a relative error of at most 0.0049.
Values may be sent and summed in bfloat16 or wider, within the bound.
No kernel may reach another device: no remote copies, remote signals or barrier semaphores. Data moves between devices by JAX's collectives and lax.ppermute only.
A program may use at most 64 MiB of HBM per device.

v0:
```python
import jax
import jax.numpy as jnp
from jax import lax
from jax.sharding import Mesh, PartitionSpec as P


def on_device(rows_in, gate_weight, up_weight, down_weight):
    width = gate_weight.shape[1]
    piece = lax.all_gather(rows_in, "hz", axis=0, tiled=True)
    piece = lax.all_gather(piece, "hy", axis=0, tiled=True)
    gate_part = jnp.dot(piece, gate_weight, preferred_element_type=jnp.float32)
    up_part = jnp.dot(piece, up_weight, preferred_element_type=jnp.float32)
    partial_value = jnp.concatenate([gate_part, up_part], axis=1)
    summed = lax.psum_scatter(partial_value, "embed", scatter_dimension=0, tiled=True)
    activated = (jax.nn.silu(summed[:, :width]) * summed[:, width:]).astype(jnp.bfloat16)
    activated = lax.all_gather(activated, "embed", axis=0, tiled=True)
    partial_out = jnp.dot(activated, down_weight, preferred_element_type=jnp.float32)
    totals = lax.psum_scatter(partial_out, "hy", scatter_dimension=0, tiled=True)
    totals = lax.psum_scatter(totals, "hz", scatter_dimension=0, tiled=True)
    return totals.astype(jnp.bfloat16)


def solution(mesh):
    embed, hidden = (mesh.shape["embed"], mesh.shape["hidden"])
    ny = {d.coords[1] for d in mesh.devices.flat}
    ny = len(ny)
    sub = Mesh(mesh.devices.reshape(embed, ny, hidden // ny), ("embed", "hy", "hz"))
    rows = P(("hy", "hz"), "embed")
    weights = P("embed", ("hy", "hz"))
    placed = (rows, weights, weights, P(("hy", "hz"), "embed"))
    return jax.shard_map(on_device, mesh=sub, in_specs=placed, out_specs=rows, check_vma=False)
```

profile of v0, /device:TPU:2, one launch (start us, length us, event | category | flops | bytes accessed | tf_op | source)
XLA Modules:
  0.0 239.4 jit_solution(16744164856222922656)
XLA Ops:
  6.5 0.0 all-gather.2.cloned.1.call-start
  6.5 31.1 %all_gather.9 = bf16[128,2048]{1,0:T(8,128)(2,1)} all-gather(bf16[16,2048]{1,0:T(8,128)(2,1)} %param.4), channel_id=1, replica_groups=mesh['embed'=8,'hy'=4,'hz'=8] {'hz'}, dimensions={0}, use_global_device_ids=true | all-gather | bytes 589824 | tf_op jit(solution)/shard_map/all_gather | solution.py:9
  37.6 0.0 all-gather.2.cloned.1.call-update
  37.7 0.0 reduce-scatter.4.cloned.1.call-start
  37.7 33.1 %all-gather.2.cloned.1.call-done = bf16[512,2048]{1,0:T(8,128)(2,1)} async-done(((bf16[128,2048]{1,0:T(8,128)(2,1)}), bf16[512,2048]{1,0:T(8,128)(2,1)}) %all-gather.2.cloned.1.call-update) | async-done | bytes 2097168 | tf_op jit(solution)/shard_map/all_gather | solution.py:10
  70.8 0.0 copy-start
  70.8 0.0 copy-start.1
  70.8 5.1 %fusion.2 = f32[512,896]{1,0:T(8,128)S(1)} fusion(bf16[512,2048]{1,0:T(8,128)(2,1)} %all-gather.2.cloned.1.call-done, bf16[2048,896]{1,0:T(8,128)(2,1)} %param.6), kind=kOutput, calls=%fused_computation.4 | convolution fusion | flops 1879048192 | bytes 7602176 | tf_op jit(solution)/shard_map/dot_general | solution.py:12
  75.9 0.0 copy-done
  75.9 0.0 copy-done.1
  76.0 2.3 fusion.1
  78.3 2.1 pad_maximum_fusion
  80.3 0.0 reduce-scatter.4.cloned.1.call-update
  80.4 0.0 reduce-scatter.6.cloned.1.call-start
  80.4 36.1 %reduce-scatter.4.cloned.1.call-done = f32[64,1792]{1,0:T(8,128)} async-done(((f32[512,1792]{1,0:T(8,128)}), f32[64,1792]{1,0:T(8,128)}) %reduce-scatter.4.cloned.1.call-update) | async-done | bytes 458768 | tf_op jit(solution)/shard_map/reduce_scatter | solution.py:14
  116.5 1.1 fusion
  117.6 15.1 %all_gather.11 = bf16[512,896]{1,0:T(8,128)(2,1)S(1)} all-gather(bf16[64,896]{1,0:T(8,128)(2,1)S(1)} %fusion), channel_id=1, replica_groups=mesh['embed'=8,'hy'=4,'hz'=8] {'embed'}, dimensions={0}, use_global_device_ids=true | all-gather | bytes 1032192 | tf_op jit(solution)/shard_map/all_gather | solution.py:16
  132.7 6.3 %fusion.3 = f32[512,2048]{1,0:T(8,128)} fusion(bf16[512,896]{1,0:T(8,128)(2,1)S(1)} %all_gather.11, bf16[896,2048]{1,0:T(8,128)(2,1)} %param.7), kind=kOutput, calls=%fused_computation.5 | convolution fusion | flops 1879048192 | bytes 8781824 | tf_op jit(solution)/shard_map/dot_general | solution.py:17
  139.0 0.0 reduce-scatter.6.cloned.1.call-update
  139.1 0.0 reduce-scatter.8.cloned.1.call-start
  139.1 51.3 %reduce-scatter.6.cloned.1.call-done = f32[128,2048]{1,0:T(8,128)} async-done(((f32[512,2048]{1,0:T(8,128)}), f32[128,2048]{1,0:T(8,128)}) %reduce-scatter.6.cloned.1.call-update) | async-done | bytes 1048592 | tf_op jit(solution)/shard_map/reduce_scatter | solution.py:18
  190.4 0.0 reduce-scatter.8.cloned.1.call-update
  190.4 40.9 %reduce-scatter.8.cloned.1.call-done = f32[16,2048]{1,0:T(8,128)} async-done(((f32[128,2048]{1,0:T(8,128)}), f32[16,2048]{1,0:T(8,128)}) %reduce-scatter.8.cloned.1.call-update) | async-done | bytes 131088 | tf_op jit(solution)/shard_map/reduce_scatter | solution.py:19
  231.4 1.5 convert_element_type.7
Async XLA Ops:
  6.5 64.2 %all-gather.2.cloned.1.call-start = ((), (), s32[]{:S(2)}) async-start(), calls=%async_computation.3 | async-start | bytes 2621440 | tf_op jit(solution)/shard_map/all_gather | solution.py:10
  37.7 78.9 %reduce-scatter.4.cloned.1.call-start = ((), (), s32[]{:S(2)}) async-start(), calls=%async_computation.4 | async-start | bytes 4128768 | tf_op jit(solution)/shard_map/reduce_scatter | solution.py:14
  70.8 5.2 %copy-start = (bf16[2048,896]{1,0:T(8,128)(2,1)S(1)}, bf16[2048,896]{1,0:T(8,128)(2,1)}, u32[]{:S(2)}) copy-start(bf16[2048,896]{1,0:T(8,128)(2,1)} %param.5) | copy-start | bytes 11010052
  70.8 5.2 %copy-start.1 = (bf16[512,2048]{1,0:T(8,128)(2,1)S(1)}, bf16[512,2048]{1,0:T(8,128)(2,1)}, u32[]{:S(2)}) copy-start(bf16[512,2048]{1,0:T(8,128)(2,1)} %all-gather.2.cloned.1.call-done) | copy-start | bytes 6291460
  80.4 110.0 %reduce-scatter.6.cloned.1.call-start = ((), (), s32[]{:S(2)}) async-start(), calls=%async_computation.5 | async-start | bytes 5242880 | tf_op jit(solution)/shard_map/reduce_scatter | solution.py:18
  139.1 92.3 %reduce-scatter.8.cloned.1.call-start = ((), (), s32[]{:S(2)}) async-start(), calls=%async_computation.6 | async-start | bytes 1179648 | tf_op jit(solution)/shard_map/reduce_scatter | solution.py:19
Sparse Core Ops, SparseCore 0:
  37.8 32.9 all-gather.1
  80.5 35.9 reduce-scatter.3
  139.2 51.1 reduce-scatter.5
  192.9 38.3 reduce-scatter.7
where the time goes:
time: 240 us; the launch traced here: 239 us
  waiting for transfers between devices  161 us (67%)
  blocking collectives  46.2 us (19%)
  matrix products  13.8 us (6%)
  between operations  13.2 us (6%)
  other arithmetic  4.72 us (2%)
    reduce_scatter x1, waiting for transfers between devices, on_device(): lax.psum_scatter(partial_out, 'hy', scatter_dimension=0, tiled=True)  51.3 us
    reduce_scatter x1, waiting for transfers between devices, on_device(): totals = lax.psum_scatter(totals, 'hz', scatter_dimension=0, tiled=True)  40.9 us
    reduce_scatter x1, waiting for transfers between devices, on_device(): lax.psum_scatter(partial_value, 'embed', scatter_dimension=0, tiled=True)  36.1 us
    all_gather x1, waiting for transfers between devices, on_device(): piece = lax.all_gather(piece, 'hy', axis=0, tiled=True)  33.1 us
    all_gather x1, blocking collectives, on_device(): piece = lax.all_gather(rows_in, 'hz', axis=0, tiled=True)  31.1 us
    all_gather x1, blocking collectives, on_device(): activated = lax.all_gather(activated, 'embed', axis=0, tiled=True)  15.1 us
    dot_general x1, matrix products, on_device(): jnp.dot(activated, down_weight, preferred_element_type=jnp.float32)  6.35 us
    dot_general x1, matrix products, on_device(): up_part = jnp.dot(piece, up_weight, preferred_element_type=jnp.float32)  5.14 us
  transfers between devices with their start and end apart: 4, of which 4 were waited for; matrix products, arithmetic and copies ran while one was open for 0% of the time, Pallas kernels for 0%

commit v1 on v0

--- a/solution.py
+++ b/solution.py
@@ -13,7 +13,9 @@
     partial_value = jnp.concatenate([gate_part, up_part], axis=1)
     summed = lax.psum_scatter(partial_value, "embed", scatter_dimension=0, tiled=True)
     activated = (jax.nn.silu(summed[:, :width]) * summed[:, width:]).astype(jnp.bfloat16)
-    activated = lax.all_gather(activated, "embed", axis=0, tiled=True)
+    activated = jnp.concatenate(
+        lax.all_to_all(jnp.stack([activated] * lax.axis_size("embed")), "embed", 0, 0), axis=0
+    )
     partial_out = jnp.dot(activated, down_weight, preferred_element_type=jnp.float32)
     totals = lax.psum_scatter(partial_out, "hy", scatter_dimension=0, tiled=True)
     totals = lax.psum_scatter(totals, "hz", scatter_dimension=0, tiled=True)

time: 240 us -> 243 us (1.012)
  blocking collectives: 46.2 us -> 50.7 us
    all_to_all x0 -> x1, blocking collectives: none -> 19.6 us  [on_device(): lax.all_to_all(jnp.stack([activated] * lax.axis_size('embed')), 'embed',...]
    all_gather x1 -> x0, blocking collectives: 15.1 us -> none  [on_device(): activated = lax.all_gather(activated, 'embed', axis=0, tiled=True)]
where the time goes in v1:
time: 243 us
  waiting for transfers between devices  160 us (66%)
  blocking collectives  50.7 us (21%)
  matrix products  13.8 us (6%)
  between operations  13.2 us (5%)
  other arithmetic  4.72 us (2%)
    reduce_scatter x1, waiting for transfers between devices, on_device(): lax.psum_scatter(partial_out, 'hy', scatter_dimension=0, tiled=True)  49.8 us
    reduce_scatter x1, waiting for transfers between devices, on_device(): totals = lax.psum_scatter(totals, 'hz', scatter_dimension=0, tiled=True)  41 us
    reduce_scatter x1, waiting for transfers between devices, on_device(): lax.psum_scatter(partial_value, 'embed', scatter_dimension=0, tiled=True)  36.1 us
    all_gather x1, waiting for transfers between devices, on_device(): piece = lax.all_gather(piece, 'hy', axis=0, tiled=True)  33.1 us
    all_gather x1, blocking collectives, on_device(): piece = lax.all_gather(rows_in, 'hz', axis=0, tiled=True)  31.1 us
    all_to_all x1, blocking collectives, on_device(): lax.all_to_all(jnp.stack([activated] * lax.axis_size('embed')), 'embed',...  19.6 us
    dot_general x1, matrix products, on_device(): jnp.dot(activated, down_weight, preferred_element_type=jnp.float32)  6.35 us
    dot_general x1, matrix products, on_device(): up_part = jnp.dot(piece, up_weight, preferred_element_type=jnp.float32)  5.14 us
  transfers between devices with their start and end apart: 4, of which 4 were waited for; matrix products, arithmetic and copies ran while one was open for 0% of the time, Pallas kernels for 0%

profile of v1, /device:TPU:2, one launch (start us, length us, event | category | flops | bytes accessed | tf_op | source)
XLA Modules:
  0.0 242.7 jit_solution(9511860883442612001)
XLA Ops:
  6.5 0.0 all-gather.2.cloned.1.call-start
  6.5 31.1 %all_gather.6 = bf16[128,2048]{1,0:T(8,128)(2,1)} all-gather(bf16[16,2048]{1,0:T(8,128)(2,1)} %param.4), channel_id=1, replica_groups=mesh['embed'=8,'hy'=4,'hz'=8] {'hz'}, dimensions={0}, use_global_device_ids=true | all-gather | bytes 589824 | tf_op jit(solution)/shard_map/all_gather | solution.py:9
  37.6 0.0 all-gather.2.cloned.1.call-update
  37.7 0.0 reduce-scatter.4.cloned.1.call-start
  37.7 33.1 %all-gather.2.cloned.1.call-done = bf16[512,2048]{1,0:T(8,128)(2,1)} async-done(((bf16[128,2048]{1,0:T(8,128)(2,1)}), bf16[512,2048]{1,0:T(8,128)(2,1)}) %all-gather.2.cloned.1.call-update) | async-done | bytes 2097168 | tf_op jit(solution)/shard_map/all_gather | solution.py:10
  70.8 0.0 copy-start
  70.8 0.0 copy-start.1
  70.8 5.1 %fusion.2 = f32[512,896]{1,0:T(8,128)S(1)} fusion(bf16[512,2048]{1,0:T(8,128)(2,1)} %all-gather.2.cloned.1.call-done, bf16[2048,896]{1,0:T(8,128)(2,1)} %param.6), kind=kOutput, calls=%fused_computation.4 | convolution fusion | flops 1879048192 | bytes 7602176 | tf_op jit(solution)/shard_map/dot_general | solution.py:12
  75.9 0.0 copy-done
  75.9 0.0 copy-done.1
  76.0 2.3 fusion.1
  78.3 2.1 pad_maximum_fusion
  80.3 0.0 reduce-scatter.4.cloned.1.call-update
  80.4 0.0 reduce-scatter.6.cloned.1.call-start
  80.4 36.1 %reduce-scatter.4.cloned.1.call-done = f32[64,1792]{1,0:T(8,128)} async-done(((f32[512,1792]{1,0:T(8,128)}), f32[64,1792]{1,0:T(8,128)}) %reduce-scatter.4.cloned.1.call-update) | async-done | bytes 458768 | tf_op jit(solution)/shard_map/reduce_scatter | solution.py:14
  116.5 1.1 fusion
  117.6 0.1 stack.2
  117.8 19.6 %all_to_all.5 = bf16[8,64,896]{2,1,0:T(8,128)(2,1)S(1)} all-to-all(bf16[8,64,896]{2,1,0:T(8,128)(2,1)S(1)} %stack.2), channel_id=1, replica_groups=mesh['embed'=8,'hy'=4,'hz'=8] {'embed'}, dimensions={0} | all-to-all | bytes 1835008 | tf_op jit(solution)/shard_map/all_to_all | solution.py:17
  137.4 6.3 %fusion.3 = f32[512,2048]{1,0:T(8,128)} fusion(bf16[512,896]{1,0:T(8,128)(2,1)S(1)} %bitcast.7, bf16[896,2048]{1,0:T(8,128)(2,1)} %param.7), kind=kOutput, calls=%fused_computation.5 | convolution fusion | flops 1879048192 | bytes 8781824 | tf_op jit(solution)/shard_map/dot_general | solution.py:19
  143.7 0.0 reduce-scatter.6.cloned.1.call-update
  143.7 0.0 reduce-scatter.8.cloned.1.call-start
  143.8 49.8 %reduce-scatter.6.cloned.1.call-done = f32[128,2048]{1,0:T(8,128)} async-done(((f32[512,2048]{1,0:T(8,128)}), f32[128,2048]{1,0:T(8,128)}) %reduce-scatter.6.cloned.1.call-update) | async-done | bytes 1048592 | tf_op jit(solution)/shard_map/reduce_scatter | solution.py:20
  193.6 0.0 reduce-scatter.8.cloned.1.call-update
  193.6 41.0 %reduce-scatter.8.cloned.1.call-done = f32[16,2048]{1,0:T(8,128)} async-done(((f32[128,2048]{1,0:T(8,128)}), f32[16,2048]{1,0:T(8,128)}) %reduce-scatter.8.cloned.1.call-update) | async-done | bytes 131088 | tf_op jit(solution)/shard_map/reduce_scatter | solution.py:21
  234.6 1.5 convert_element_type.7
Async XLA Ops:
  6.5 64.2 %all-gather.2.cloned.1.call-start = ((), (), s32[]{:S(2)}) async-start(), calls=%async_computation.4 | async-start | bytes 2621440 | tf_op jit(solution)/shard_map/all_gather | solution.py:10
  37.7 78.9 %reduce-scatter.4.cloned.1.call-start = ((), (), s32[]{:S(2)}) async-start(), calls=%async_computation.5 | async-start | bytes 4128768 | tf_op jit(solution)/shard_map/reduce_scatter | solution.py:14
  70.8 5.2 %copy-start = (bf16[2048,896]{1,0:T(8,128)(2,1)S(1)}, bf16[2048,896]{1,0:T(8,128)(2,1)}, u32[]{:S(2)}) copy-start(bf16[2048,896]{1,0:T(8,128)(2,1)} %param.5) | copy-start | bytes 11010052
  70.8 5.2 %copy-start.1 = (bf16[512,2048]{1,0:T(8,128)(2,1)S(1)}, bf16[512,2048]{1,0:T(8,128)(2,1)}, u32[]{:S(2)}) copy-start(bf16[512,2048]{1,0:T(8,128)(2,1)} %all-gather.2.cloned.1.call-done) | copy-start | bytes 6291460
  80.4 113.2 %reduce-scatter.6.cloned.1.call-start = ((), (), s32[]{:S(2)}) async-start(), calls=%async_computation.6 | async-start | bytes 5242880 | tf_op jit(solution)/shard_map/reduce_scatter | solution.py:20
  143.7 90.9 %reduce-scatter.8.cloned.1.call-start = ((), (), s32[]{:S(2)}) async-start(), calls=%async_computation.7 | async-start | bytes 1179648 | tf_op jit(solution)/shard_map/reduce_scatter | solution.py:21
Sparse Core Ops, SparseCore 0:
  37.8 32.9 all-gather.1
  80.5 35.9 reduce-scatter.3
  143.9 49.7 reduce-scatter.5
  196.2 38.3 reduce-scatter.7
